TPU v7x, 256 devices: a whole 4x4x8 slice. The times are simulated.
256 devices in a mesh: ka: 64 (over z, y, core), pb: 4 (over x).
Axes of the slice: x: 4, y: 4, z: 8, core: 2. Of those that a mesh axis runs over, the one named last changes fastest.
Arguments:
- occupation: float32 [6, 262144], P(None, 'ka'), may hold values from 0 to 1
- gain_table: bfloat16 [64, 36, 262144], P('pb', None, 'ka'), may hold values from 0.0049743652 to 0.19921875
- loss_table: bfloat16 [64, 36, 262144], P('pb', None, 'ka'), may hold values from 0.0049743652 to 0.19921875
- owner: int32 [4, 64, 16, 32, 1], P('pb', 'ka'), may hold values from 0 to 63; in each aligned block of 512 rows (0 to 511, 512 to 1023, ..., all dimensions but the last counted through in order) at most 16 rows name the same one
- local_index: int32 [4, 64, 16, 32], P('pb', 'ka'), may hold values from 0 to 31
- pair_mask: int32 [64, 36], P('pb'), may hold values 0 or 1
- counts: int32 [4, 64], P('pb', 'ka'), may hold values from 1 to 16, as said below
Outputs:
- collision: float32 [6, 262144], P(None, ('ka', 'pb'))
- section_occupation: float32 [6, 262144], P(None, ('ka', 'pb'))
Inputs may be any that keep to these rules, and one draw needn't show every extreme that they name: Among the 16 x 32 entries of one q-shift group and one k-block, no owner is named more than 16 times. The active q-shifts of a group at a k-block are its first counts ones.
All inputs are finite; a program needn't handle non-finite values. No bound on the sum of `pair_mask` on one device may be relied on, other than what follows from the above.
Results may differ from a plain program's by a relative error of at most 0.0003.
Values sent between devices are 32-bit elements; how exact they have to be, the bound alone decides.
No kernel may reach another device: no remote copies, remote signals or barrier semaphores. Data moves between devices by JAX's collectives and lax.ppermute only.
A program may use at most 128 MiB of HBM per device.

v0:
```python
import jax
import jax.numpy as jnp
from jax import lax
from jax.sharding import PartitionSpec as P

half_step = 0.5


def body(occupation, gain_table, loss_table, owner, local_index, pair_mask, counts):
    bands, width = occupation.shape
    shifts = gain_table.shape[0]
    sub_count = local_index.shape[3]
    sub_width = width // sub_count
    ka_count = lax.axis_size("ka")
    total_requests = shifts * sub_count
    owners = owner.reshape(total_requests)
    sources = local_index.reshape(total_requests)
    whole = lax.all_gather(occupation, "ka", axis=1, tiled=True)
    pieces = whole.reshape(bands, ka_count * sub_count, sub_width)
    picked = jnp.take(pieces, owners * sub_count + sources, axis=1).transpose(1, 0, 2)
    shifted = (
        picked.reshape(shifts, sub_count, bands, sub_width)
        .transpose(0, 2, 1, 3)
        .reshape(shifts, bands, width)
    )
    active = (jnp.arange(shifts, dtype=jnp.int32) < counts.reshape(())).astype(jnp.float32)
    weight = pair_mask.astype(jnp.float32) * active[:, None]
    gain_four = (gain_table.astype(jnp.float32) * weight[:, :, None]).reshape(
        shifts, bands, bands, width
    )
    loss_four = (loss_table.astype(jnp.float32) * weight[:, :, None]).reshape(
        shifts, bands, bands, width
    )
    inflow = jnp.einsum("smnk,snk->mk", gain_four, shifted)
    outflow = jnp.einsum("smnk,snk->mk", loss_four, 1.0 - shifted)
    partial_terms = (1.0 - occupation) * inflow - occupation * outflow
    collision = lax.psum_scatter(partial_terms, "pb", scatter_dimension=1, tiled=True)
    share_width = collision.shape[1]
    own_share = lax.dynamic_slice_in_dim(
        occupation, lax.axis_index("pb") * share_width, share_width, 1
    )
    return (collision, own_share + half_step * collision)


def solution(mesh):
    return jax.shard_map(
        body,
        mesh=mesh,
        in_specs=(
            P(None, "ka"),
            P("pb", None, "ka"),
            P("pb", None, "ka"),
            P("pb", "ka", None, None, None),
            P("pb", "ka", None, None),
            P("pb", None),
            P("pb", "ka"),
        ),
        out_specs=(P(None, ("ka", "pb")), P(None, ("ka", "pb"))),
        check_vma=False,
    )
```

profile of v0, /device:TPU:8, one launch (start us, length us, event | category | flops | bytes accessed | tf_op | source)
XLA Modules:
  0.0 143.5 jit_solution(18443966641634054089)
XLA Ops:
  7.2 0.0 all-gather.2.cloned.1.call-start
  7.2 0.7 all-gather.2.cloned.1.call-update
  7.9 0.0 reduce-scatter.2.cloned.1.call-start
  7.9 0.8 reshape.77
  8.7 0.8 reshape.75
  9.5 0.7 fusion.1
  10.2 0.1 mul.61
  10.3 0.1 mul.60
  11.0 0.8 convert_multiply_fusion.2
  11.8 0.1 copy.10
  11.9 13.3 %convert_multiply_fusion.1 = (f32[16,36,4096]{2,0,1:T(8,128)}, f32[16,36,4096]{2,0,1:T(8,128)}) fusion(bf16[16,36,4096]{2,0,1:T(8,128)(2,1)} %param.8, f32[16,36]{0,1:T(8,128)S(1)} %copy.10, bf16[16,36,4096]{2,0,1:T(8,128)(2,1)} %param.9), kind=kLoop, calls=%fused_computation.4 | loop fusion | flops 9437184 | bytes 28313856 | tf_op jit(solution)/shard_map/mul | solution.py:28
  25.2 70.2 %all-gather.2.cloned.1.call-done = f32[6,262144]{1,0:T(8,128)} async-done(((f32[6,4096]{1,0:T(8,128)}), f32[6,262144]{1,0:T(8,128)}) %all-gather.2.cloned.1.call-update) | async-done | bytes 6291472 | tf_op jit(solution)/shard_map/all_gather | solution.py:18
  95.4 4.4 %gather_fusion = f32[512,6,128]{2,1,0:T(8,128)S(1)} fusion(f32[6,2048,128]{2,0,1:T(8,128)} %bitcast.36, s32[1024]{0:T(1024)S(1)} %pad_clamp_fusion), kind=kCustom, calls=%fused_computation | custom fusion | bytes 3147776 | tf_op jit(solution)/shard_map/jit(_take)/gather | solution.py:20
  99.8 1.7 %broadcast_select_fusion = f32[512,6,128]{2,1,0:T(8,128)S(1)} fusion(f32[512,6,128]{2,1,0:T(8,128)S(1)} %gather_fusion, pred[512]{0:T(512)(128)(4,1)S(1)} %compare_and_fusion), kind=kLoop, calls=%fused_computation.6 | loop fusion | flops 393216 | bytes 3146240 | tf_op jit(solution)/shard_map/jit(_take)/select_n | solution.py:20
  101.6 0.2 subtract_bitcast_fusion
  101.8 0.9 copy.24
  102.7 0.9 copy.23
  103.6 0.0 copy-start
  103.7 9.4 %multiply_reduce_fusion = (f32[4096,6]{0,1:T(8,128)S(1)}, f32[4096,6]{0,1:T(8,128)S(1)}) fusion(f32[4096,6,16,6]{0,2,1,3:T(8,128)} %bitcast.33, f32[4096,6,16]{0,2,1:T(8,128)S(1)} %copy.24, f32[4096,6,16,6]{0,2,1,3:T(8,128)} %bitcast.32, f32[4096,6,16]{0,2,1:T(8,128)S(1)} %copy.23), kind=kLoop, calls=%fused_computation.1 | loop fusion | flops 9388032 | bytes 22216704 | tf_op jit(solution)/shard_map/smnk,snk->mk/dot_general | solution.py:35
  113.1 0.0 copy-done
  113.1 0.7 fusion
  113.7 0.0 reduce-scatter.2.cloned.1.call-update
  113.8 21.5 %reduce-scatter.2.cloned.1.call-done = f32[6,1024]{1,0:T(8,128)} async-done(((f32[6,4096]{1,0:T(8,128)}), f32[6,1024]{1,0:T(8,128)}) %reduce-scatter.2.cloned.1.call-update) | async-done | bytes 24592 | tf_op jit(solution)/shard_map/reduce_scatter | solution.py:37
  135.3 1.4 multiply_add_fusion
  (4 shorter events, 0.0 us)
Async XLA Ops:
  7.2 88.3 %all-gather.2.cloned.1.call-start = ((), (), s32[]{:S(2)}) async-start(), calls=%async_computation.1 | async-start | bytes 8519680 | tf_op jit(solution)/shard_map/all_gather | solution.py:18
  7.9 127.4 %reduce-scatter.2.cloned.1.call-start = ((), (), s32[]{:S(2)}) async-start(), calls=%async_computation.2 | async-start | bytes 163840 | tf_op jit(solution)/shard_map/reduce_scatter | solution.py:37
  103.6 9.4 %copy-start = (f32[6,4096]{1,0:T(8,128)S(1)}, f32[6,4096]{1,0:T(8,128)}, u32[]{:S(2)}) copy-start(f32[6,4096]{1,0:T(8,128)} %param.7) | copy-start | bytes 294916
Sparse Core Ops, SparseCore 0:
  10.8 84.6 all-gather.1
  113.9 21.3 reduce-scatter.1
where the time goes:
time: 144 us; the launch traced here: 143 us
  waiting for transfers between devices  92.4 us (64%)
  other arithmetic  28.2 us (20%)
  between operations  14.8 us (10%)
  local copies, waits for them, and re-layouts  7.99 us (6%)
    all_gather x1, waiting for transfers between devices, body(): whole = lax.all_gather(occupation, 'ka', axis=1, tiled=True)  70.2 us
    reduce_scatter x1, waiting for transfers between devices, body(): lax.psum_scatter(partial_terms, 'pb', scatter_dimension=1, tiled=True)  21.5 us
    mul x1, other arithmetic, body(): gain_table.astype(jnp.float32) * weight[:, :, None]  13.3 us
    dot_general x1, other arithmetic, body(): outflow = jnp.einsum('smnk,snk->mk', loss_four, 1.0 - shifted)  9.4 us
    gather x1, local copies, waits for them, and re-layouts, body(): jnp.take(pieces, owners * sub_count + sources, axis=1).transpose(1, 0, 2)  4.36 us
  transfers between devices with their start and end apart: 2, of which 2 were waited for; matrix products, arithmetic and copies ran while one was open for 12% of the time, Pallas kernels for 0%

commit v1 on v0

--- a/solution.py
+++ b/solution.py
@@ -15,7 +15,15 @@
     total_requests = shifts * sub_count
     owners = owner.reshape(total_requests)
     sources = local_index.reshape(total_requests)
-    whole = lax.all_gather(occupation, "ka", axis=1, tiled=True)
+    whole = jnp.concatenate(
+        lax.all_to_all(
+            jnp.stack([occupation for _ in range(lax.axis_size("ka"))], 0),
+            concat_axis=0,
+            split_axis=0,
+            axis_name="ka",
+        ),
+        1,
+    )
     pieces = whole.reshape(bands, ka_count * sub_count, sub_width)
     picked = jnp.take(pieces, owners * sub_count + sources, axis=1).transpose(1, 0, 2)
     shifted = (

time: 144 us -> 258 us (1.79)
  waiting for transfers between devices: 92.4 us -> 192 us
  starting transfers between devices: 0.08 us -> 12.5 us
  local copies, waits for them, and re-layouts: 7.99 us -> 11.8 us
    all_to_all x0 -> x1, waiting for transfers between devices: none -> 170 us  [body(): lax.all_to_all(jnp.stack([occupation for _ in range(lax.axis_size('ka'))]...]
    all_gather x1 -> x0, waiting for transfers between devices: 70.2 us -> none  [body(): whole = lax.all_gather(occupation, 'ka', axis=1, tiled=True)]
    all_to_all x0 -> x1, starting transfers between devices: none -> 12.4 us  [body(): lax.all_to_all(jnp.stack([occupation for _ in range(lax.axis_size('ka'))]...]
    another operation x0 -> x1, local copies, waits for them, and re-layouts: none -> 5.19 us  [body(): jnp.stack([occupation for _ in range(lax.axis_size('ka'))], 0)]
  transfers between devices with their start and end apart: 2 -> 2, of which waited for: 2 -> 2; matrix products, arithmetic and copies ran while one was open for 12% -> 5% of each run, Pallas kernels for 0% -> 0%
where the time goes in v1:
time: 258 us
  waiting for transfers between devices  192 us (74%)
  other arithmetic  26.8 us (10%)
  between operations  14.8 us (6%)
  starting transfers between devices  12.5 us (5%)
  local copies, waits for them, and re-layouts  11.8 us (5%)
    all_to_all x1, waiting for transfers between devices, body(): lax.all_to_all(jnp.stack([occupation for _ in range(lax.axis_size('ka'))]...  170 us
    reduce_scatter x1, waiting for transfers between devices, body(): lax.psum_scatter(partial_terms, 'pb', scatter_dimension=1, tiled=True)  21.3 us
    mul x1, other arithmetic, body(): gain_table.astype(jnp.float32) * weight[:, :, None]  13.3 us
    all_to_all x1, starting transfers between devices, body(): lax.all_to_all(jnp.stack([occupation for _ in range(lax.axis_size('ka'))]...  12.4 us
    dot_general x1, other arithmetic, body(): outflow = jnp.einsum('smnk,snk->mk', loss_four, 1.0 - shifted)  9.4 us
    another operation x1, local copies, waits for them, and re-layouts, body(): jnp.stack([occupation for _ in range(lax.axis_size('ka'))], 0)  5.19 us
  transfers between devices with their start and end apart: 2, of which 2 were waited for; matrix products, arithmetic and copies ran while one was open for 5% of the time, Pallas kernels for 0%

profile of v1, /device:TPU:8, one launch (start us, length us, event | category | flops | bytes accessed | tf_op | source)
XLA Modules:
  0.0 257.6 jit_solution(12326985874030446899)
XLA Ops:
  7.2 5.2 %stack.2 = f32[64,6,4096]{2,1,0:T(8,128)} broadcast(f32[6,4096]{1,0:T(8,128)} %param.7), dimensions={1,2} | broadcast | bytes 6389760 | tf_op jit(solution)/shard_map/stack | solution.py:20
  12.4 0.0 copy-start.1
  12.4 0.0 copy-start.2
  12.4 0.0 copy-start.3
  12.4 12.4 %all-to-all-start = ((f32[64,6,4096]{2,1,0:T(8,128)}), f32[64,6,4096]{2,1,0:T(8,128)}, u32[]{:S(2)}, u32[]{:S(2)}) async-start(f32[64,6,4096]{2,1,0:T(8,128)} %stack.2), calls=%async_computation | async-start | bytes 16777216 | tf_op jit(solution)/shard_map/all_to_all | solution.py:19
  24.8 0.0 reduce-scatter.2.cloned.1.call-start
  24.8 0.0 copy-done.1
  24.8 0.1 reshape.79
  24.9 0.1 reshape.77
  25.0 0.0 copy-done.2
  25.0 0.1 mul.61
  25.1 0.1 mul.60
  25.9 0.0 copy-done.3
  25.9 0.1 convert_multiply_fusion.2
  25.9 0.1 copy.14
  26.1 13.3 %convert_multiply_fusion.1 = (f32[16,36,4096]{2,0,1:T(8,128)}, f32[16,36,4096]{2,0,1:T(8,128)}) fusion(bf16[16,36,4096]{2,0,1:T(8,128)(2,1)} %param.8, f32[16,36]{0,1:T(8,128)S(1)} %copy.14, bf16[16,36,4096]{2,0,1:T(8,128)(2,1)} %param.9), kind=kLoop, calls=%fused_computation.4 | loop fusion | flops 9437184 | bytes 28313856 | tf_op jit(solution)/shard_map/mul | solution.py:36
  39.3 170.5 %all-to-all-done = f32[64,6,4096]{2,1,0:T(8,128)} async-done(((f32[64,6,4096]{2,1,0:T(8,128)}), f32[64,6,4096]{2,1,0:T(8,128)}, u32[]{:S(2)}, u32[]{:S(2)}) %all-to-all-start) | async-done | bytes 6291488 | tf_op jit(solution)/shard_map/all_to_all | solution.py:19
  209.8 4.4 %gather_fusion = f32[512,6,128]{2,1,0:T(8,128)S(1)} fusion(f32[6,2048,128]{2,0,1:T(8,128)} %bitcast.5, s32[1024]{0:T(1024)S(1)} %pad_clamp_fusion), kind=kCustom, calls=%fused_computation | custom fusion | bytes 3147776 | tf_op jit(solution)/shard_map/jit(_take)/gather | solution.py:28
  214.2 1.7 broadcast_select_fusion
  215.9 0.2 subtract_bitcast_fusion
  216.2 0.9 copy.28
  217.1 0.9 copy.27
  218.0 0.0 copy-start
  218.0 9.4 %multiply_reduce_fusion = (f32[4096,6]{0,1:T(8,128)S(1)}, f32[4096,6]{0,1:T(8,128)S(1)}) fusion(f32[4096,6,16,6]{0,2,1,3:T(8,128)} %bitcast.35, f32[4096,6,16]{0,2,1:T(8,128)S(1)} %copy.28, f32[4096,6,16,6]{0,2,1,3:T(8,128)} %bitcast.34, f32[4096,6,16]{0,2,1:T(8,128)S(1)} %copy.27), kind=kLoop, calls=%fused_computation.1 | loop fusion | flops 9388032 | bytes 22216704 | tf_op jit(solution)/shard_map/smnk,snk->mk/dot_general | solution.py:43
  227.4 0.0 copy-done
  227.4 0.7 fusion
  228.1 0.0 reduce-scatter.2.cloned.1.call-update
  228.1 21.3 %reduce-scatter.2.cloned.1.call-done = f32[6,1024]{1,0:T(8,128)} async-done(((f32[6,4096]{1,0:T(8,128)}), f32[6,1024]{1,0:T(8,128)}) %reduce-scatter.2.cloned.1.call-update) | async-done | bytes 24592 | tf_op jit(solution)/shard_map/reduce_scatter | solution.py:45
  249.4 1.4 multiply_add_fusion
  (5 shorter events, 0.1 us)
Async XLA Ops:
  12.4 12.5 %copy-start.1 = (s32[1,1,16,32]{3,2,1,0:T(8,128)S(1)}, s32[1,1,16,32]{3,2,1,0:T(8,128)}, u32[]{:S(2)}) copy-start(s32[1,1,16,32]{3,2,1,0:T(8,128)} %param.11) | copy-start | bytes 6148
  12.4 12.7 %copy-start.2 = (s32[1,1,16,32,1]{3,4,2,1,0:T(1,128)S(1)}, s32[1,1,16,32,1]{3,4,2,1,0:T(1,128)}, u32[]{:S(2)}) copy-start(s32[1,1,16,32,1]{3,4,2,1,0:T(1,128)} %param.10) | copy-start | bytes 6148
  12.4 13.5 %copy-start.3 = (s32[16,36]{1,0:T(8,128)S(1)}, s32[16,36]{1,0:T(8,128)}, u32[]{:S(2)}) copy-start(s32[16,36]{1,0:T(8,128)} %param.12) | copy-start | bytes 6916
  12.4 197.4 %all-to-all-start = ((f32[64,6,4096]{2,1,0:T(8,128)}), f32[64,6,4096]{2,1,0:T(8,128)}, u32[]{:S(2)}, u32[]{:S(2)}) async-start(f32[64,6,4096]{2,1,0:T(8,128)} %stack.2), calls=%async_computation | async-start | bytes 16777216 | tf_op jit(solution)/shard_map/all_to_all | solution.py:19
  24.8 224.6 %reduce-scatter.2.cloned.1.call-start = ((), (), s32[]{:S(2)}) async-start(), calls=%async_computation.2 | async-start | bytes 163840 | tf_op jit(solution)/shard_map/reduce_scatter | solution.py:45
  218.0 9.4 %copy-start = (f32[6,4096]{1,0:T(8,128)S(1)}, f32[6,4096]{1,0:T(8,128)}, u32[]{:S(2)}) copy-start(f32[6,4096]{1,0:T(8,128)} %param.7) | copy-start | bytes 294916
Sparse Core Ops, SparseCore 0:
  228.2 21.1 reduce-scatter.1
